TPU v7x, 256 devices: a whole 4x4x8 slice. The times are simulated.
256 devices in a mesh: dp: 16 (over z_lo, x, core), fsdp: 16 (over y, z_hi).
Axes of the slice: x: 4, y: 4, z: 8 (z_hi: 4, z_lo: 2; z = z_hi * 2 + z_lo), core: 2. Of those that a mesh axis runs over, the one named last changes fastest.
Arguments:
- hidden_in: bfloat16 [131072, 1536], P(('dp', 'fsdp')), may hold values from -6 to 6
- grad_out: bfloat16 [131072, 1536], P(('dp', 'fsdp')), may hold values from -6 to 6
- lengths: int32 [256, 3], P(('dp', 'fsdp')), may hold values from 1 to 510, as said below
- conv_kernel: float32 [5, 1536], replicated, may hold values from -3 to 3
- norm_gain: float32 [1536], replicated, may hold values from 0.5 to 2
- out_weight: bfloat16 [1536, 1536], P('fsdp'), may hold values from -0.15625 to 0.15625
Outputs:
- output: float32 [131072, 1536], P(('dp', 'fsdp'))
- grad_hidden: float32 [131072, 1536], P(('dp', 'fsdp'))
- grad_weight: float32 [1536, 1536], P('fsdp')
- grad_kernel: float32 [5, 1536], replicated
- grad_gain: float32 [1536], replicated
Inputs may be any that keep to these rules, and one draw needn't show every extreme that they name: `lengths`: each row sums to at most 512. A row whose sum exceeds (3) * 128 sums to exactly 512, holds 2 utterances of length 1 followed by one of length 510, and then the row with the same fsdp index whose dp index differs by half the dp axis sums to at most (2) * 128; every other row sums to at most (3) * 128. Some row in every draw sums to 512.
All inputs are finite; a program needn't handle non-finite values.
Results may differ from a plain program's by a relative error of at most 0.003.
Values may be sent and summed in bfloat16 or wider, within the bound.
No kernel may reach another device: no remote copies, remote signals or barrier semaphores. Data moves between devices by JAX's collectives and lax.ppermute only.
A program may use at most 128 MiB of HBM per device.

v0:
```python
import math
import jax
import jax.numpy as jnp
from jax import lax
from jax.sharding import PartitionSpec as P


def tap_mask(lengths, frames, count):
    utt_ends = jnp.cumsum(lengths)
    position = jnp.arange(frames, dtype=jnp.int32)
    segment_id = jnp.sum((position[:, None] >= utt_ends[None, :]).astype(jnp.int32), axis=1)
    inside = position < utt_ends[-1]
    half_width = count // 2
    segment_pad = jnp.pad(segment_id, half_width, constant_values=-1)
    inside_pad = jnp.pad(inside, half_width, constant_values=False)
    rows_out = []
    for k in range(count):
        same = (segment_pad[k : k + frames] == segment_id) & inside_pad[k : k + frames] & inside
        rows_out.append(same.astype(jnp.float32))
    return jnp.stack(rows_out)


def shifted(x, half_width):
    frames = x.shape[0]
    padded = jnp.pad(x, ((half_width, half_width), (0, 0)))
    return [padded[k : k + frames] for k in range(2 * half_width + 1)]


def butterfly(x, axis):
    size = lax.axis_size(axis)
    step = 1
    while step < size:
        pairs = [(i, i ^ step) for i in range(size)]
        x = x + lax.ppermute(x, axis, pairs)
        step *= 2
    return x


def shards(hidden_in, grad_out, lengths, conv_kernel, norm_gain, out_weight):
    frames, chans = hidden_in.shape
    count = conv_kernel.shape[0]
    half_width = count // 2
    full_weight = lax.all_gather(out_weight, "fsdp", axis=0, tiled=True)
    taps = tap_mask(lengths[0], frames, count)
    live = taps[half_width][:, None]
    views = shifted(hidden_in, half_width)
    mixed = jnp.zeros((frames, chans), jnp.float32)
    for k in range(count):
        mixed = mixed + conv_kernel[k] * views[k].astype(jnp.float32) * taps[k][:, None]
    centred = mixed - jnp.mean(mixed, axis=-1, keepdims=True)
    inverse = lax.rsqrt(jnp.mean(centred * centred, axis=-1, keepdims=True) + 1e-05)
    normed = centred * inverse
    scaled = normed * norm_gain
    squash = jax.nn.sigmoid(scaled)
    activation = (scaled * squash * live).astype(jnp.bfloat16)
    weight_terms = lax.dot_general(
        activation, grad_out, (((0,), (0,)), ((), ())), preferred_element_type=jnp.float32
    )
    shard_sum = lax.psum_scatter(weight_terms, "fsdp", scatter_dimension=0, tiled=True)
    output = jnp.dot(activation, full_weight, preferred_element_type=jnp.float32)
    grad_act = lax.dot_general(
        grad_out, full_weight, (((1,), (1,)), ((), ())), preferred_element_type=jnp.float32
    )
    grad_scaled = grad_act * live * squash * (1.0 + scaled * (1.0 - squash))
    gain_grad = jnp.sum(grad_scaled * normed, axis=0)
    grad_normed = grad_scaled * norm_gain
    grad_mixed = inverse * (
        grad_normed
        - jnp.mean(grad_normed, axis=-1, keepdims=True)
        - normed * jnp.mean(grad_normed * normed, axis=-1, keepdims=True)
    )
    kernel_rows = []
    for k in range(count):
        weighted = grad_mixed * taps[k][:, None]
        kernel_rows.append(jnp.sum(weighted * views[k].astype(jnp.float32), axis=0))
    back_views = shifted(grad_mixed, half_width)
    grad_hidden = jnp.zeros((frames, chans), jnp.float32)
    for k in range(count):
        grad_hidden = grad_hidden + conv_kernel[k] * (
            back_views[count - 1 - k] * taps[count - 1 - k][:, None]
        )
    small = jnp.concatenate([jnp.stack(kernel_rows), gain_grad[None]], axis=0)
    small = butterfly(small, "fsdp")
    total = butterfly(jnp.concatenate([shard_sum, small], axis=0), "dp")
    rows = shard_sum.shape[0]
    dp_count = lax.axis_size("dp")
    fsdp_count = lax.axis_size("fsdp")
    factor = 1.0 / math.sqrt(frames * dp_count * fsdp_count)
    weight_sum = total[:rows] * factor
    kernel_sum = total[rows : rows + count] * factor
    gain_sum = total[rows + count] * factor
    return (output, grad_hidden, weight_sum, kernel_sum, gain_sum)


def solution(mesh):
    placed = (
        P(("dp", "fsdp"), None),
        P(("dp", "fsdp"), None),
        P(("dp", "fsdp"), None),
        P(),
        P(),
        P("fsdp", None),
    )
    return jax.shard_map(
        shards,
        mesh=mesh,
        in_specs=placed,
        out_specs=(P(("dp", "fsdp"), None), P(("dp", "fsdp"), None), P("fsdp", None), P(), P()),
        check_vma=False,
    )
```

profile of v0, /device:TPU:2, one launch (start us, length us, event | category | flops | bytes accessed | tf_op | source)
XLA Modules:
  0.0 291.9 jit_solution(425887298165945984)
XLA Ops:
  7.2 0.0 copy-start
  7.2 0.0 all-gather.2.cloned.1.call-start
  7.2 0.7 all-gather.2.cloned.1.call-update
  7.9 0.0 reduce-scatter.2.cloned.1.call-start
  8.0 0.8 reduce-window.4
  8.8 0.6 slice.88
  9.4 0.6 iota_compare_fusion.1
  10.0 0.1 convert_reduce_fusion
  10.1 1.1 slice_reduce_fusion.4
  11.2 0.7 and_convert_fusion.4
  11.9 0.0 copy-start.6
  11.9 8.6 %fusion.28 = (f32[512]{0:T(512)S(1)}, f32[512,1536]{1,0:T(8,128)S(1)}) fusion(f32[512]{0:T(512)S(1)} %get-tuple-element.24, f32[1536]{0:T(1024)S(1)} %get-tuple-element.16, f32[512]{0:T(512)S(1)} %get-tuple-element.22, f32[1536]{0:T(1024)S(1)} %get-tuple-element.17, f32[512]{0:T(512)S(1)} %get-tuple-element.26, bf16[512,1536]{1,0:T(8,128)(2,1)} %param.6, ...), kind=kLoop, calls=%fused_computation.80 | loop fusion | flops 15728128 | bytes 4761600 | tf_op jit(solution)/shard_map/reduce_sum | solution.py:50
  20.5 0.0 copy-start.1
  20.5 0.4 multiply_reduce_fusion.2
  21.0 1.2 copy-done.1
  22.2 0.0 copy-done
  22.2 0.0 copy-done.6
  22.2 5.4 %fusion.26 = f32[1536,1536]{1,0:T(8,128)} fusion(bf16[512,1536]{1,0:T(8,128)(2,1)S(1)} %copy-done, f32[512,1536]{1,0:T(8,128)S(1)} %get-tuple-element.20, f32[1536]{0:T(1024)S(1)} %copy-done.6, f32[512]{0:T(512)S(1)} %add_rsqrt_fusion, f32[512]{0:T(512)S(1)} %broadcast_multiply_fusion.2, f32[512]{0:T(512)S(1)} %get-tuple-element.26), kind=kOutput, calls=%fused_computation.78 | convolution fusion | flops 2422996992 | bytes 14168064 | tf_op jit(solution)/shard_map/dot_general | solution.py:56
  27.6 0.0 reduce-scatter.2.cloned.1.call-update
  27.7 0.0 copy-start.5
  27.7 64.1 %all-gather.2.cloned.1.call-done = bf16[1536,1536]{1,0:T(8,128)(2,1)} async-done(((bf16[96,1536]{1,0:T(8,128)(2,1)}), bf16[1536,1536]{1,0:T(8,128)(2,1)}) %all-gather.2.cloned.1.call-update) | async-done | bytes 4718608 | tf_op jit(solution)/shard_map/all_gather | solution.py:43
  91.8 0.0 copy-start.2
  91.8 7.1 %multiply_reduce_fusion = (f32[1536]{0:T(1024)S(1)}, f32[512]{0:T(512)S(1)}, f32[512]{0:T(512)S(1)}, f32[512,1536]{1,0:T(8,128)S(1)}) fusion(f32[512,1536]{1,0:T(8,128)} %copy-done.1, f32[512]{0:T(512)S(1)} %add_rsqrt_fusion, f32[512]{0:T(512)S(1)} %broadcast_multiply_fusion.2, f32[1536]{0:T(1024)S(1)} %copy-done.6, f32[512]{0:T(512)S(1)} %get-tuple-element.26, ...), kind=kOutput, calls=%fused_computation.27 | convolution fusion | flops 2430072320 | bytes 12605440 | tf_op jit(solution)/shard_map/dot_general | solution.py:61
  99.0 0.0 copy-done.5
  99.0 0.0 copy-done.2
  99.0 5.8 %fusion.15 = (f32[1536]{0:T(1024)S(1)}, f32[1536]{0:T(1024)S(1)}, f32[1536]{0:T(1024)S(1)}, f32[1536]{0:T(1024)S(1)}, f32[1536]{0:T(1024)S(1)}, /*index=5*/f32[512,1536]{1,0:T(8,128)}) fusion(f32[512]{0:T(512)S(1)} %get-tuple-element.24, bf16[512,1536]{1,0:T(8,128)(2,1)S(1)} %copy-done.5, f32[512]{0:T(512)S(1)} %get-tuple-element.22, ...), kind=kLoop, calls=%fused_computation.26 | loop fusion | flops 21225984 | bytes 11065344 | tf_op jit(solution)/shard_map/reduce_sum | solution.py:75
  104.8 0.1 concatenate.6
  104.9 6.4 %collective-permute-start = (f32[6,1536]{1,0:T(8,128)S(1)}, f32[6,1536]{1,0:T(8,128)S(1)}, u32[]{:S(2)}, u32[]{:S(2)}) collective-permute-start(f32[6,1536]{1,0:T(8,128)S(1)} %concatenate.6), channel_id=1, source_target_pairs={{0,1},{1,0},{2,3},{3,2},{4,5},{5,4},{6,7},{7,6},{8,9},{9,8},{10,11... | collective-permute-start | bytes 110600 | tf_op jit(solution)/shard_map/ppermute | solution.py:34
  111.3 6.6 %collective-permute-done = f32[6,1536]{1,0:T(8,128)S(1)} collective-permute-done((f32[6,1536]{1,0:T(8,128)S(1)}, f32[6,1536]{1,0:T(8,128)S(1)}, u32[]{:S(2)}, u32[]{:S(2)}) %collective-permute-start) | collective-permute-done | bytes 36896 | tf_op jit(solution)/shard_map/ppermute | solution.py:34
  117.9 0.1 collective-permute-start.1
  118.0 11.7 %collective-permute-done.1 = f32[6,1536]{1,0:T(8,128)S(1)} collective-permute-done((f32[6,1536]{1,0:T(8,128)S(1)}, f32[6,1536]{1,0:T(8,128)S(1)}, u32[]{:S(2)}, u32[]{:S(2)}) %collective-permute-start.1) | collective-permute-done | bytes 36896 | tf_op jit(solution)/shard_map/ppermute | solution.py:34
  129.7 1.5 collective-permute-start.2
  131.3 3.6 %collective-permute-done.2 = f32[6,1536]{1,0:T(8,128)S(1)} collective-permute-done((f32[6,1536]{1,0:T(8,128)S(1)}, f32[6,1536]{1,0:T(8,128)S(1)}, u32[]{:S(2)}, u32[]{:S(2)}) %collective-permute-start.2) | collective-permute-done | bytes 36896 | tf_op jit(solution)/shard_map/ppermute | solution.py:34
  134.9 3.0 %collective-permute-start.3 = (f32[6,1536]{1,0:T(8,128)S(1)}, f32[6,1536]{1,0:T(8,128)S(1)}, u32[]{:S(2)}, u32[]{:S(2)}) collective-permute-start(f32[6,1536]{1,0:T(8,128)S(1)} %add.87), channel_id=1, source_target_pairs={{0,8},{1,9},{2,10},{3,11},{4,12},{5,13},{6,14},{7,15},{8,0},{9,1},... | collective-permute-start | bytes 110600 | tf_op jit(solution)/shard_map/ppermute | solution.py:34
  137.8 3.2 %collective-permute-done.3 = f32[6,1536]{1,0:T(8,128)S(1)} collective-permute-done((f32[6,1536]{1,0:T(8,128)S(1)}, f32[6,1536]{1,0:T(8,128)S(1)}, u32[]{:S(2)}, u32[]{:S(2)}) %collective-permute-start.3) | collective-permute-done | bytes 36896 | tf_op jit(solution)/shard_map/ppermute | solution.py:34
  141.0 88.5 %reduce-scatter.2.cloned.1.call-done = f32[96,1536]{1,0:T(8,128)} async-done(((f32[1536,1536]{1,0:T(8,128)}), f32[96,1536]{1,0:T(8,128)}) %reduce-scatter.2.cloned.1.call-update) | async-done | bytes 589840 | tf_op jit(solution)/shard_map/reduce_scatter | solution.py:59
  229.5 0.0 copy-start.3
  229.5 1.3 pad_maximum_fusion
  230.8 0.3 collective-permute-start.4
  231.0 2.1 collective-permute-done.4
  233.1 1.2 fusion.25
  234.3 0.5 collective-permute-start.5
  234.8 16.0 %collective-permute-done.5 = f32[102,1536]{1,0:T(8,128)S(1)} collective-permute-done((f32[102,1536]{1,0:T(8,128)S(1)}, f32[102,1536]{1,0:T(8,128)S(1)}, u32[]{:S(2)}, u32[]{:S(2)}) %collective-permute-start.5) | collective-permute-done | bytes 626720 | tf_op jit(solution)/shard_map/ppermute | solution.py:34
  250.8 0.1 add.90
  250.9 2.2 collective-permute-start.6
  253.1 0.0 copy-done.3
  253.1 0.0 copy-start.4
  253.1 7.1 %fusion.27 = f32[512,1536]{1,0:T(8,128)} fusion(bf16[1536,1536]{1,0:T(8,128)(2,1)} %all-gather.2.cloned.1.call-done, f32[512,1536]{1,0:T(8,128)S(1)} %copy-done.3, f32[1536]{0:T(1024)S(1)} %copy-done.6, f32[512]{0:T(512)S(1)} %add_rsqrt_fusion, f32[512]{0:T(512)S(1)} %broadcast_multiply_fusion.2, f32[512]{0:T(512)S(1)} %get-tuple-element.26), kind=kOutput, calls=%fused_computation.79 | convolution fusion | flops 2422996992 | bytes 11022336 | tf_op jit(solution)/shard_map/dot_general | solution.py:60
  260.1 7.9 %collective-permute-done.6 = f32[102,1536]{1,0:T(8,128)S(1)} collective-permute-done((f32[102,1536]{1,0:T(8,128)S(1)}, f32[102,1536]{1,0:T(8,128)S(1)}, u32[]{:S(2)}, u32[]{:S(2)}) %collective-permute-start.6) | collective-permute-done | bytes 626720 | tf_op jit(solution)/shard_map/ppermute | solution.py:34
  268.0 0.1 add.91
  268.1 1.1 collective-permute-start.7
  269.2 0.0 copy-done.4
  269.2 4.0 %multiply_add_fusion = f32[512,1536]{1,0:T(8,128)} fusion(f32[512,1536]{1,0:T(8,128)S(1)} %copy-done.4, f32[512]{0:T(512)S(1)} %get-tuple-element.24, f32[1536]{0:T(1024)S(1)} %get-tuple-element.16, f32[512]{0:T(512)S(1)} %get-tuple-element.22, f32[1536]{0:T(1024)S(1)} %get-tuple-element.17, f32[512]{0:T(512)S(1)} %get-tuple-element.26, ...), kind=kLoop, calls=%fused_computation.28 | loop fusion | flops 11010048 | bytes 6332416 | tf_op jit(solution)/shard_map/add | solution.py:79
  273.2 9.7 %collective-permute-done.7 = f32[102,1536]{1,0:T(8,128)S(1)} collective-permute-done((f32[102,1536]{1,0:T(8,128)S(1)}, f32[102,1536]{1,0:T(8,128)S(1)}, u32[]{:S(2)}, u32[]{:S(2)}) %collective-permute-start.7) | collective-permute-done | bytes 626720 | tf_op jit(solution)/shard_map/ppermute | solution.py:34
  282.9 0.1 add.92
  283.0 0.9 slice_multiply_fusion
  283.8 0.6 slice_multiply_fusion.1
  284.5 0.6 fusion.16
  (14 shorter events, 0.1 us)
Async XLA Ops:
  7.2 15.0 %copy-start = (bf16[512,1536]{1,0:T(8,128)(2,1)S(1)}, bf16[512,1536]{1,0:T(8,128)(2,1)}, u32[]{:S(2)}) copy-start(bf16[512,1536]{1,0:T(8,128)(2,1)} %param.7) | copy-start | bytes 4718596
  7.2 84.6 %all-gather.2.cloned.1.call-start = ((), (), s32[]{:S(2)}) async-start(), calls=%async_computation.1 | async-start | bytes 5013504 | tf_op jit(solution)/shard_map/all_gather | solution.py:43
  7.9 221.6 %reduce-scatter.2.cloned.1.call-start = ((), (), s32[]{:S(2)}) async-start(), calls=%async_computation.2 | async-start | bytes 10027008 | tf_op jit(solution)/shard_map/reduce_scatter | solution.py:59
  11.9 10.3 %copy-start.6 = (f32[1536]{0:T(1024)S(1)}, f32[1536]{0:T(1024)}, u32[]{:S(2)}) copy-start(f32[1536]{0:T(1024)} %param.10) | copy-start | bytes 18436
  20.5 1.7 copy-start.1
  27.7 71.3 %copy-start.5 = (bf16[512,1536]{1,0:T(8,128)(2,1)S(1)}, bf16[512,1536]{1,0:T(8,128)(2,1)}, u32[]{:S(2)}) copy-start(bf16[512,1536]{1,0:T(8,128)(2,1)} %param.6) | copy-start | bytes 4718596
  91.8 7.2 %copy-start.2 = (f32[512,1536]{1,0:T(8,128)S(1)}, f32[512,1536]{1,0:T(8,128)}, u32[]{:S(2)}) copy-start(f32[512,1536]{1,0:T(8,128)} %copy-done.1) | copy-start | bytes 9437188
  104.9 13.0 %collective-permute-start = (f32[6,1536]{1,0:T(8,128)S(1)}, f32[6,1536]{1,0:T(8,128)S(1)}, u32[]{:S(2)}, u32[]{:S(2)}) collective-permute-start(f32[6,1536]{1,0:T(8,128)S(1)} %concatenate.6), channel_id=1, source_target_pairs={{0,1},{1,0},{2,3},{3,2},{4,5},{5,4},{6,7},{7,6},{8,9},{9,8},{10,11... | collective-permute-start | bytes 110600 | tf_op jit(solution)/shard_map/ppermute | solution.py:34
  117.9 11.8 %collective-permute-start.1 = (f32[6,1536]{1,0:T(8,128)S(1)}, f32[6,1536]{1,0:T(8,128)S(1)}, u32[]{:S(2)}, u32[]{:S(2)}) collective-permute-start(f32[6,1536]{1,0:T(8,128)S(1)} %add.85), channel_id=1, source_target_pairs={{0,2},{1,3},{2,0},{3,1},{4,6},{5,7},{6,4},{7,5},{8,10},{9,11},{10,... | collective-permute-start | bytes 110600 | tf_op jit(solution)/shard_map/ppermute | solution.py:34
  129.7 5.1 %collective-permute-start.2 = (f32[6,1536]{1,0:T(8,128)S(1)}, f32[6,1536]{1,0:T(8,128)S(1)}, u32[]{:S(2)}, u32[]{:S(2)}) collective-permute-start(f32[6,1536]{1,0:T(8,128)S(1)} %add.86), channel_id=1, source_target_pairs={{0,4},{1,5},{2,6},{3,7},{4,0},{5,1},{6,2},{7,3},{8,12},{9,13},{10,... | collective-permute-start | bytes 110600 | tf_op jit(solution)/shard_map/ppermute | solution.py:34
  134.9 6.2 %collective-permute-start.3 = (f32[6,1536]{1,0:T(8,128)S(1)}, f32[6,1536]{1,0:T(8,128)S(1)}, u32[]{:S(2)}, u32[]{:S(2)}) collective-permute-start(f32[6,1536]{1,0:T(8,128)S(1)} %add.87), channel_id=1, source_target_pairs={{0,8},{1,9},{2,10},{3,11},{4,12},{5,13},{6,14},{7,15},{8,0},{9,1},... | collective-permute-start | bytes 110600 | tf_op jit(solution)/shard_map/ppermute | solution.py:34
  229.5 23.6 %copy-start.3 = (f32[512,1536]{1,0:T(8,128)S(1)}, f32[512,1536]{1,0:T(8,128)}, u32[]{:S(2)}) copy-start(f32[512,1536]{1,0:T(8,128)} %copy-done.1) | copy-start | bytes 9437188
  230.8 2.3 collective-permute-start.4
  234.3 16.5 %collective-permute-start.5 = (f32[102,1536]{1,0:T(8,128)S(1)}, f32[102,1536]{1,0:T(8,128)S(1)}, u32[]{:S(2)}, u32[]{:S(2)}) collective-permute-start(f32[102,1536]{1,0:T(8,128)S(1)} %fusion.25), channel_id=1, source_target_pairs={{0,32},{16,48},{32,0},{48,16},{64,96},{80,112},{96,64},{112,80},{1... | collective-permute-start | bytes 1880072 | tf_op jit(solution)/shard_map/ppermute | solution.py:34
  250.9 17.2 %collective-permute-start.6 = (f32[102,1536]{1,0:T(8,128)S(1)}, f32[102,1536]{1,0:T(8,128)S(1)}, u32[]{:S(2)}, u32[]{:S(2)}) collective-permute-start(f32[102,1536]{1,0:T(8,128)S(1)} %add.90), channel_id=1, source_target_pairs={{0,64},{16,80},{32,96},{48,112},{64,0},{80,16},{96,32},{112,48},{1... | collective-permute-start | bytes 1880072 | tf_op jit(solution)/shard_map/ppermute | solution.py:34
  253.1 16.1 %copy-start.4 = (f32[512,1536]{1,0:T(8,128)S(1)}, f32[512,1536]{1,0:T(8,128)}, u32[]{:S(2)}) copy-start(f32[512,1536]{1,0:T(8,128)} %get-tuple-element.18) | copy-start | bytes 9437188
  268.1 14.8 %collective-permute-start.7 = (f32[102,1536]{1,0:T(8,128)S(1)}, f32[102,1536]{1,0:T(8,128)S(1)}, u32[]{:S(2)}, u32[]{:S(2)}) collective-permute-start(f32[102,1536]{1,0:T(8,128)S(1)} %add.91), channel_id=1, source_target_pairs={{0,128},{16,144},{32,160},{48,176},{64,192},{80,208},{96,224},{112... | collective-permute-start | bytes 1880072 | tf_op jit(solution)/shard_map/ppermute | solution.py:34
Sparse Core Ops, SparseCore 0:
  10.5 81.2 all-gather.1
  95.6 133.8 reduce-scatter.1
where the time goes:
time: 292 us
  waiting for transfers between devices  214 us (73%)
  other arithmetic  25.9 us (9%)
  matrix products  19.6 us (7%)
  starting transfers between devices  15.1 us (5%)
  between operations  14.2 us (5%)
  local copies, waits for them, and re-layouts  3 us (1%)
    reduce_scatter x1, waiting for transfers between devices, shards(): lax.psum_scatter(weight_terms, 'fsdp', scatter_dimension=0, tiled=True)  88.5 us
    all_gather x1, waiting for transfers between devices, shards(): full_weight = lax.all_gather(out_weight, 'fsdp', axis=0, tiled=True)  64.1 us
    ppermute x8, waiting for transfers between devices, butterfly(): x = x + lax.ppermute(x, axis, pairs)  60.7 us
    ppermute x8, starting transfers between devices, butterfly(): x = x + lax.ppermute(x, axis, pairs)  15.1 us
    reduce_sum x1, other arithmetic, shards(): centred = mixed - jnp.mean(mixed, axis=-1, keepdims=True)  8.57 us
    dot_general x1, matrix products, shards(): lax.dot_general(grad_out, full_weight, (((1,), (1,)), ((), ())), preferre...  7.13 us
    dot_general x1, matrix products, shards(): jnp.dot(activation, full_weight, preferred_element_type=jnp.float32)  7.06 us
  transfers between devices with their start and end apart: 10, of which 10 were waited for; matrix products, arithmetic and copies ran while one was open for 15% of the time, Pallas kernels for 0%

commit v1 on v0

--- a/solution.py
+++ b/solution.py
@@ -40,7 +40,9 @@
     frames, chans = hidden_in.shape
     count = conv_kernel.shape[0]
     half_width = count // 2
-    full_weight = lax.all_gather(out_weight, "fsdp", axis=0, tiled=True)
+    full_weight = jnp.concatenate(
+        lax.all_to_all(jnp.stack([out_weight] * lax.axis_size("fsdp")), "fsdp", 0, 0), axis=0
+    )
     taps = tap_mask(lengths[0], frames, count)
     live = taps[half_width][:, None]
     views = shifted(hidden_in, half_width)

time: 292 us -> 323 us (1.11)
  blocking collectives: 0 us -> 155 us
  waiting for transfers between devices: 214 us -> 89.1 us
  matrix products: 19.6 us -> 16.2 us
    all_to_all x0 -> x1, blocking collectives: none -> 155 us  [shards(): lax.all_to_all(jnp.stack([out_weight] * lax.axis_size('fsdp')), 'fsdp', 0...]
    all_gather x1 -> x0, waiting for transfers between devices: 64.1 us -> none  [shards(): full_weight = lax.all_gather(out_weight, 'fsdp', axis=0, tiled=True)]
    reduce_scatter x1, waiting for transfers between devices: 88.5 us -> 36.8 us  [shards(): lax.psum_scatter(weight_terms, 'fsdp', scatter_dimension=0, tiled=True)]
    ppermute x8, waiting for transfers between devices: 60.7 us -> 52.3 us  [butterfly(): x = x + lax.ppermute(x, axis, pairs)]
    dot_general x1, matrix products: 7.13 us -> 3.71 us  [shards(): lax.dot_general(grad_out, full_weight, (((1,), (1,)), ((), ())), preferre...]
  transfers between devices with their start and end apart: 10 -> 9, of which waited for: 10 -> 9; matrix products, arithmetic and copies ran while one was open for 15% -> 7% of each run, Pallas kernels for 0% -> 0%
where the time goes in v1:
time: 323 us; the launch traced here: 322 us
  blocking collectives  155 us (48%)
  waiting for transfers between devices  89.1 us (28%)
  other arithmetic  25.4 us (8%)
  starting transfers between devices  17.7 us (5%)
  matrix products  16.2 us (5%)
  between operations  14.2 us (4%)
  local copies, waits for them, and re-layouts  4.39 us (1%)
    all_to_all x1, blocking collectives, shards(): lax.all_to_all(jnp.stack([out_weight] * lax.axis_size('fsdp')), 'fsdp', 0...  155 us
    ppermute x8, waiting for transfers between devices, butterfly(): x = x + lax.ppermute(x, axis, pairs)  52.3 us
    reduce_scatter x1, waiting for transfers between devices, shards(): lax.psum_scatter(weight_terms, 'fsdp', scatter_dimension=0, tiled=True)  36.8 us
    ppermute x8, starting transfers between devices, butterfly(): x = x + lax.ppermute(x, axis, pairs)  17.7 us
    reduce_sum x1, other arithmetic, shards(): centred = mixed - jnp.mean(mixed, axis=-1, keepdims=True)  8.57 us
    dot_general x1, matrix products, shards(): jnp.dot(activation, full_weight, preferred_element_type=jnp.float32)  7.11 us
  transfers between devices with their start and end apart: 9, of which 9 were waited for; matrix products, arithmetic and copies ran while one was open for 7% of the time, Pallas kernels for 0%

profile of v1, /device:TPU:2, one launch (start us, length us, event | category | flops | bytes accessed | tf_op | source)
XLA Modules:
  0.0 322.5 jit_solution(12618182744964249653)
XLA Ops:
  7.2 0.0 copy-start
  7.2 0.0 reduce-scatter.2.cloned.1.call-start
  7.2 0.9 reduce-window.4
  8.2 0.6 slice.88
  8.7 0.6 iota_compare_fusion.1
  9.4 0.1 convert_reduce_fusion
  9.5 1.1 slice_reduce_fusion.4
  10.6 0.1 and_convert_fusion.4
  10.7 0.0 copy-start.8
  10.7 8.6 %fusion.28 = (f32[512]{0:T(512)S(1)}, f32[512,1536]{1,0:T(8,128)S(1)}) fusion(f32[512]{0:T(512)S(1)} %get-tuple-element.24, f32[1536]{0:T(1024)S(1)} %get-tuple-element.16, f32[512]{0:T(512)S(1)} %get-tuple-element.22, f32[1536]{0:T(1024)S(1)} %get-tuple-element.17, f32[512]{0:T(512)S(1)} %get-tuple-element.27, bf16[512,1536]{1,0:T(8,128)(2,1)} %param.6, ...), kind=kLoop, calls=%fused_computation.80 | loop fusion | flops 15728128 | bytes 4761600 | tf_op jit(solution)/shard_map/reduce_sum | solution.py:52
  19.2 0.0 copy-start.1
  19.3 0.4 multiply_reduce_fusion.2
  19.7 1.2 copy-done.1
  20.9 0.0 copy-done
  20.9 0.0 copy-done.8
  20.9 5.4 %fusion.26 = f32[1536,1536]{1,0:T(8,128)} fusion(bf16[512,1536]{1,0:T(8,128)(2,1)S(1)} %copy-done, f32[512,1536]{1,0:T(8,128)S(1)} %get-tuple-element.20, f32[1536]{0:T(1024)S(1)} %copy-done.8, f32[512]{0:T(512)S(1)} %add_rsqrt_fusion, f32[512]{0:T(512)S(1)} %broadcast_multiply_fusion.2, f32[512]{0:T(512)S(1)} %get-tuple-element.27), kind=kOutput, calls=%fused_computation.78 | convolution fusion | flops 2422996992 | bytes 14168064 | tf_op jit(solution)/shard_map/dot_general | solution.py:58
  26.3 0.0 copy-start.7
  26.3 0.0 reduce-scatter.2.cloned.1.call-update
  26.4 0.9 copy-done.7
  27.3 0.4 stack.12
  27.7 0.0 copy-start.2
  27.8 155.5 %all_to_all.5 = bf16[16,96,1536]{2,1,0:T(8,128)(2,1)S(1)} all-to-all(bf16[16,96,1536]{2,1,0:T(8,128)(2,1)S(1)} %stack.12), channel_id=1, replica_groups=mesh['dp'=16,'fsdp'=16] {'fsdp'}, dimensions={0} | all-to-all | bytes 9437184 | tf_op jit(solution)/shard_map/all_to_all | solution.py:44
  183.2 0.0 copy-start.6
  183.2 0.0 copy-done.2
  183.2 0.0 copy-start.5
  183.2 3.7 %multiply_reduce_fusion = (f32[1536]{0:T(1024)S(1)}, f32[512]{0:T(512)S(1)}, f32[512]{0:T(512)S(1)}, f32[512,1536]{1,0:T(8,128)S(1)}) fusion(f32[512,1536]{1,0:T(8,128)S(1)} %copy-done.2, f32[512]{0:T(512)S(1)} %add_rsqrt_fusion, f32[512]{0:T(512)S(1)} %broadcast_multiply_fusion.2, f32[1536]{0:T(1024)S(1)} %copy-done.8, f32[512]{0:T(512)S(1)} %get-tuple-element.27, ...), kind=kOutput, calls=%fused_computation.27 | convolution fusion | flops 2430072320 | bytes 12605440 | tf_op jit(solution)/shard_map/dot_general | solution.py:63
  186.9 0.0 copy-done.6
  187.0 0.0 copy-done.5
  187.0 5.8 %fusion.15 = (f32[1536]{0:T(1024)S(1)}, f32[1536]{0:T(1024)S(1)}, f32[1536]{0:T(1024)S(1)}, f32[1536]{0:T(1024)S(1)}, f32[1536]{0:T(1024)S(1)}, /*index=5*/f32[512,1536]{1,0:T(8,128)}) fusion(f32[512]{0:T(512)S(1)} %get-tuple-element.24, bf16[512,1536]{1,0:T(8,128)(2,1)S(1)} %copy-done.5, f32[512]{0:T(512)S(1)} %get-tuple-element.22, ...), kind=kLoop, calls=%fused_computation.26 | loop fusion | flops 21225984 | bytes 11065344 | tf_op jit(solution)/shard_map/reduce_sum | solution.py:77
  192.8 0.1 concatenate.6
  192.9 2.5 collective-permute-start
  195.4 4.6 %collective-permute-done = f32[6,1536]{1,0:T(8,128)S(1)} collective-permute-done((f32[6,1536]{1,0:T(8,128)S(1)}, f32[6,1536]{1,0:T(8,128)S(1)}, u32[]{:S(2)}, u32[]{:S(2)}) %collective-permute-start) | collective-permute-done | bytes 36896 | tf_op jit(solution)/shard_map/ppermute | solution.py:34
  200.0 3.0 collective-permute-start.1
  203.0 7.5 %collective-permute-done.1 = f32[6,1536]{1,0:T(8,128)S(1)} collective-permute-done((f32[6,1536]{1,0:T(8,128)S(1)}, f32[6,1536]{1,0:T(8,128)S(1)}, u32[]{:S(2)}, u32[]{:S(2)}) %collective-permute-start.1) | collective-permute-done | bytes 36896 | tf_op jit(solution)/shard_map/ppermute | solution.py:34
  210.5 3.3 %collective-permute-start.2 = (f32[6,1536]{1,0:T(8,128)S(1)}, f32[6,1536]{1,0:T(8,128)S(1)}, u32[]{:S(2)}, u32[]{:S(2)}) collective-permute-start(f32[6,1536]{1,0:T(8,128)S(1)} %add.86), channel_id=1, source_target_pairs={{0,4},{1,5},{2,6},{3,7},{4,0},{5,1},{6,2},{7,3},{8,12},{9,13},{10,... | collective-permute-start | bytes 110600 | tf_op jit(solution)/shard_map/ppermute | solution.py:34
  213.8 2.4 collective-permute-done.2
  216.2 4.9 %collective-permute-start.3 = (f32[6,1536]{1,0:T(8,128)S(1)}, f32[6,1536]{1,0:T(8,128)S(1)}, u32[]{:S(2)}, u32[]{:S(2)}) collective-permute-start(f32[6,1536]{1,0:T(8,128)S(1)} %add.87), channel_id=1, source_target_pairs={{0,8},{1,9},{2,10},{3,11},{4,12},{5,13},{6,14},{7,15},{8,0},{9,1},... | collective-permute-start | bytes 110600 | tf_op jit(solution)/shard_map/ppermute | solution.py:34
  221.1 2.4 collective-permute-done.3
  223.5 36.8 %reduce-scatter.2.cloned.1.call-done = f32[96,1536]{1,0:T(8,128)} async-done(((f32[1536,1536]{1,0:T(8,128)}), f32[96,1536]{1,0:T(8,128)}) %reduce-scatter.2.cloned.1.call-update) | async-done | bytes 589840 | tf_op jit(solution)/shard_map/reduce_scatter | solution.py:61
  260.3 0.0 copy-start.3
  260.3 1.3 pad_maximum_fusion
  261.5 0.1 collective-permute-start.4
  261.6 2.1 collective-permute-done.4
  263.7 1.1 fusion.25
  264.8 0.5 collective-permute-start.5
  265.4 16.0 %collective-permute-done.5 = f32[102,1536]{1,0:T(8,128)S(1)} collective-permute-done((f32[102,1536]{1,0:T(8,128)S(1)}, f32[102,1536]{1,0:T(8,128)S(1)}, u32[]{:S(2)}, u32[]{:S(2)}) %collective-permute-start.5) | collective-permute-done | bytes 626720 | tf_op jit(solution)/shard_map/ppermute | solution.py:34
  281.3 0.1 add.90
  281.4 2.1 collective-permute-start.6
  283.5 0.0 copy-done.3
  283.5 0.0 copy-start.4
  283.6 7.1 %fusion.27 = f32[512,1536]{1,0:T(8,128)} fusion(bf16[1536,1536]{1,0:T(8,128)(2,1)} %bitcast.9, f32[512,1536]{1,0:T(8,128)S(1)} %copy-done.3, f32[1536]{0:T(1024)S(1)} %copy-done.8, f32[512]{0:T(512)S(1)} %add_rsqrt_fusion, f32[512]{0:T(512)S(1)} %broadcast_multiply_fusion.2, f32[512]{0:T(512)S(1)} %get-tuple-element.27), kind=kOutput, calls=%fused_computation.79 | convolution fusion | flops 2422996992 | bytes 11022336 | tf_op jit(solution)/shard_map/dot_general | solution.py:62
  290.7 7.9 %collective-permute-done.6 = f32[102,1536]{1,0:T(8,128)S(1)} collective-permute-done((f32[102,1536]{1,0:T(8,128)S(1)}, f32[102,1536]{1,0:T(8,128)S(1)}, u32[]{:S(2)}, u32[]{:S(2)}) %collective-permute-start.6) | collective-permute-done | bytes 626720 | tf_op jit(solution)/shard_map/ppermute | solution.py:34
  298.6 0.1 add.91
  298.7 1.2 collective-permute-start.7
  299.8 0.0 copy-done.4
  299.9 4.1 %multiply_add_fusion = f32[512,1536]{1,0:T(8,128)} fusion(f32[512,1536]{1,0:T(8,128)S(1)} %copy-done.4, f32[512]{0:T(512)S(1)} %get-tuple-element.24, f32[1536]{0:T(1024)S(1)} %get-tuple-element.16, f32[512]{0:T(512)S(1)} %get-tuple-element.22, f32[1536]{0:T(1024)S(1)} %get-tuple-element.17, f32[512]{0:T(512)S(1)} %get-tuple-element.27, ...), kind=kLoop, calls=%fused_computation.28 | loop fusion | flops 11010048 | bytes 6332416 | tf_op jit(solution)/shard_map/add | solution.py:81
  303.9 9.5 %collective-permute-done.7 = f32[102,1536]{1,0:T(8,128)S(1)} collective-permute-done((f32[102,1536]{1,0:T(8,128)S(1)}, f32[102,1536]{1,0:T(8,128)S(1)}, u32[]{:S(2)}, u32[]{:S(2)}) %collective-permute-start.7) | collective-permute-done | bytes 626720 | tf_op jit(solution)/shard_map/ppermute | solution.py:34
  313.5 0.1 add.92
  313.5 0.9 slice_multiply_fusion
  314.4 0.6 slice_multiply_fusion.1
  315.0 0.6 fusion.16
  (14 shorter events, 0.1 us)
Async XLA Ops:
  7.2 13.7 %copy-start = (bf16[512,1536]{1,0:T(8,128)(2,1)S(1)}, bf16[512,1536]{1,0:T(8,128)(2,1)}, u32[]{:S(2)}) copy-start(bf16[512,1536]{1,0:T(8,128)(2,1)} %param.7) | copy-start | bytes 4718596
  7.2 253.1 %reduce-scatter.2.cloned.1.call-start = ((), (), s32[]{:S(2)}) async-start(), calls=%async_computation.2 | async-start | bytes 10027008 | tf_op jit(solution)/shard_map/reduce_scatter | solution.py:61
  10.7 10.2 %copy-start.8 = (f32[1536]{0:T(1024)S(1)}, f32[1536]{0:T(1024)}, u32[]{:S(2)}) copy-start(f32[1536]{0:T(1024)} %param.10) | copy-start | bytes 18436
  19.2 1.7 copy-start.1
  26.3 1.0 copy-start.7
  27.7 155.5 %copy-start.2 = (f32[512,1536]{1,0:T(8,128)S(1)}, f32[512,1536]{1,0:T(8,128)}, u32[]{:S(2)}) copy-start(f32[512,1536]{1,0:T(8,128)} %copy-done.1) | copy-start | bytes 9437188
  183.2 3.7 %copy-start.6 = (bf16[16,96,1536]{2,1,0:T(8,128)(2,1)}, bf16[16,96,1536]{2,1,0:T(8,128)(2,1)S(1)}, u32[]{:S(2)}) copy-start(bf16[16,96,1536]{2,1,0:T(8,128)(2,1)S(1)} %all_to_all.5) | copy-start | bytes 14155780
  183.2 3.7 %copy-start.5 = (bf16[512,1536]{1,0:T(8,128)(2,1)S(1)}, bf16[512,1536]{1,0:T(8,128)(2,1)}, u32[]{:S(2)}) copy-start(bf16[512,1536]{1,0:T(8,128)(2,1)} %param.6) | copy-start | bytes 4718596
  192.9 7.1 %collective-permute-start = (f32[6,1536]{1,0:T(8,128)S(1)}, f32[6,1536]{1,0:T(8,128)S(1)}, u32[]{:S(2)}, u32[]{:S(2)}) collective-permute-start(f32[6,1536]{1,0:T(8,128)S(1)} %concatenate.6), channel_id=1, source_target_pairs={{0,1},{1,0},{2,3},{3,2},{4,5},{5,4},{6,7},{7,6},{8,9},{9,8},{10,11... | collective-permute-start | bytes 110600 | tf_op jit(solution)/shard_map/ppermute | solution.py:34
  200.0 10.5 %collective-permute-start.1 = (f32[6,1536]{1,0:T(8,128)S(1)}, f32[6,1536]{1,0:T(8,128)S(1)}, u32[]{:S(2)}, u32[]{:S(2)}) collective-permute-start(f32[6,1536]{1,0:T(8,128)S(1)} %add.85), channel_id=1, source_target_pairs={{0,2},{1,3},{2,0},{3,1},{4,6},{5,7},{6,4},{7,5},{8,10},{9,11},{10,... | collective-permute-start | bytes 110600 | tf_op jit(solution)/shard_map/ppermute | solution.py:34
  210.5 5.7 %collective-permute-start.2 = (f32[6,1536]{1,0:T(8,128)S(1)}, f32[6,1536]{1,0:T(8,128)S(1)}, u32[]{:S(2)}, u32[]{:S(2)}) collective-permute-start(f32[6,1536]{1,0:T(8,128)S(1)} %add.86), channel_id=1, source_target_pairs={{0,4},{1,5},{2,6},{3,7},{4,0},{5,1},{6,2},{7,3},{8,12},{9,13},{10,... | collective-permute-start | bytes 110600 | tf_op jit(solution)/shard_map/ppermute | solution.py:34
  216.2 7.3 %collective-permute-start.3 = (f32[6,1536]{1,0:T(8,128)S(1)}, f32[6,1536]{1,0:T(8,128)S(1)}, u32[]{:S(2)}, u32[]{:S(2)}) collective-permute-start(f32[6,1536]{1,0:T(8,128)S(1)} %add.87), channel_id=1, source_target_pairs={{0,8},{1,9},{2,10},{3,11},{4,12},{5,13},{6,14},{7,15},{8,0},{9,1},... | collective-permute-start | bytes 110600 | tf_op jit(solution)/shard_map/ppermute | solution.py:34
  260.3 23.3 %copy-start.3 = (f32[512,1536]{1,0:T(8,128)S(1)}, f32[512,1536]{1,0:T(8,128)}, u32[]{:S(2)}) copy-start(f32[512,1536]{1,0:T(8,128)} %copy-done.1) | copy-start | bytes 9437188
  261.5 2.2 collective-permute-start.4
  264.8 16.5 %collective-permute-start.5 = (f32[102,1536]{1,0:T(8,128)S(1)}, f32[102,1536]{1,0:T(8,128)S(1)}, u32[]{:S(2)}, u32[]{:S(2)}) collective-permute-start(f32[102,1536]{1,0:T(8,128)S(1)} %fusion.25), channel_id=1, source_target_pairs={{0,32},{16,48},{32,0},{48,16},{64,96},{80,112},{96,64},{112,80},{1... | collective-permute-start | bytes 1880072 | tf_op jit(solution)/shard_map/ppermute | solution.py:34
  281.4 17.2 %collective-permute-start.6 = (f32[102,1536]{1,0:T(8,128)S(1)}, f32[102,1536]{1,0:T(8,128)S(1)}, u32[]{:S(2)}, u32[]{:S(2)}) collective-permute-start(f32[102,1536]{1,0:T(8,128)S(1)} %add.90), channel_id=1, source_target_pairs={{0,64},{16,80},{32,96},{48,112},{64,0},{80,16},{96,32},{112,48},{1... | collective-permute-start | bytes 1880072 | tf_op jit(solution)/shard_map/ppermute | solution.py:34
  283.5 16.3 %copy-start.4 = (f32[512,1536]{1,0:T(8,128)S(1)}, f32[512,1536]{1,0:T(8,128)}, u32[]{:S(2)}) copy-start(f32[512,1536]{1,0:T(8,128)} %get-tuple-element.18) | copy-start | bytes 9437188
  298.7 14.8 %collective-permute-start.7 = (f32[102,1536]{1,0:T(8,128)S(1)}, f32[102,1536]{1,0:T(8,128)S(1)}, u32[]{:S(2)}, u32[]{:S(2)}) collective-permute-start(f32[102,1536]{1,0:T(8,128)S(1)} %add.91), channel_id=1, source_target_pairs={{0,128},{16,144},{32,160},{48,176},{64,192},{80,208},{96,224},{112... | collective-permute-start | bytes 1880072 | tf_op jit(solution)/shard_map/ppermute | solution.py:34
Sparse Core Ops, SparseCore 0:
  26.5 233.7 reduce-scatter.1
